TPU v7x, 256 devices: a whole 4x4x8 slice. The times are simulated.
256 devices in a mesh: row: 32 (over x, z), col: 8 (over y, core).
Axes of the slice: x: 4, y: 4, z: 8, core: 2. Of those that a mesh axis runs over, the one named last changes fastest.
Arguments:
- points: float32 [16384, 256], P('row'), may hold values from -6 to 6
- nugget: float32 [16384], P('row'), may hold values from 0.5 to 2
- weights: float32 [256], replicated, may hold values from 0.0005 to 0.005
- band_start: int32 [32], replicated, may hold values from 0 to 30, as said below
Outputs:
- factored: float32 [32, 4, 8, 512, 512], P('row', None, 'col')
Inputs may be any that keep to these rules, and one draw needn't show every extreme that they name: band_start[i] <= i - 1 for every i >= 1, band_start[0] = 0; band_start[17] = 0; the last tile row has band_start = 30.
All inputs are finite; a program needn't handle non-finite values.
Results may differ from a plain program's by a relative error of at most 0.0003.
Values sent between devices are 32-bit elements; how exact they have to be, the bound alone decides.
No kernel may reach another device: no remote copies, remote signals or barrier semaphores. Data moves between devices by JAX's collectives and lax.ppermute only.
A program may use at most 128 MiB of HBM per device.

v0:
```python
import jax
import jax.numpy as jnp
from jax import lax
from jax.sharding import PartitionSpec as P


def broadcast(value, axis, source):
    kept = jnp.where(lax.axis_index(axis) == source, value, 0).astype(value.dtype)
    return lax.psum(kept, axis)


def kernel_tile(xrow, xcol, weights):
    weighted = xrow * weights
    sq_row = jnp.sum(weighted * xrow, axis=1)
    sq_col = jnp.sum(xcol * xcol * weights, axis=1)
    cross = jnp.dot(
        weighted, xcol.T, precision=lax.Precision.HIGHEST, preferred_element_type=jnp.float32
    )
    dist_sq = jnp.maximum(sq_row[:, None] + sq_col[None, :] - 2.0 * cross, 0.0)
    dist = jnp.sqrt(3.0 * dist_sq)
    return (1.0 + dist) * jnp.exp(-dist)


def factor_panel(local, p, n_col, my_row):
    owner_col = p % n_col
    diag_tile = broadcast(local, "row", p)
    lpp = jnp.linalg.cholesky(diag_tile)
    solved = jax.scipy.linalg.solve_triangular(lpp, local.T, lower=True).T
    panel = broadcast(solved, "col", owner_col)
    panel = jnp.where(my_row > p, panel, jnp.where(my_row == p, lpp, jnp.float32(0.0)))
    return panel


def column_factors(panel, my_col, n_col, blocks):
    width = panel.shape[1]
    slab = panel.shape[0] // (n_col * blocks)
    mixed = lax.all_to_all(panel, "row", split_axis=0, concat_axis=0, tiled=True)
    picked = lax.dynamic_slice_in_dim(mixed.reshape(blocks, n_col, slab, width), my_col, 1, 1)
    picked = picked.reshape(blocks, slab, width)
    whole = lax.all_gather(picked, "row", axis=1, tiled=True)
    return [whole[k] for k in range(blocks)]


def apply_panel(tiles, panel, col_tiles, p, my_row, my_col, n_col):
    result = []
    for k in range(len(tiles)):
        column = my_col + n_col * k
        prod = jnp.dot(
            panel,
            col_tiles[k].T,
            precision=lax.Precision.HIGHEST,
            preferred_element_type=jnp.float32,
        )
        live = (column > p) & (column <= my_row)
        block = tiles[k] - jnp.where(live, prod, jnp.float32(0.0))
        result.append(jnp.where(column == p, panel, block))
    return result


def body(points, nugget, weights, band_start):
    n_row = lax.axis_size("row")
    n_col = lax.axis_size("col")
    blocks = n_row // n_col
    my_row = lax.axis_index("row")
    my_col = lax.axis_index("col")
    diag_nugget = jnp.diag(nugget)
    tiles = []
    for k in range(blocks):
        column = my_col + n_col * k
        xcol = broadcast(points, "row", column)
        block = kernel_tile(points, xcol, weights)
        keep = (column >= band_start[my_row]) & (column <= my_row)
        block = jnp.where(keep, block, jnp.float32(0.0))
        tiles.append(block + jnp.where(column == my_row, diag_nugget, jnp.float32(0.0)))
    for p in range(2):
        panel = factor_panel(tiles[p // n_col], p, n_col, my_row)
        col_tiles = column_factors(panel, my_col, n_col, blocks)
        tiles = apply_panel(tiles, panel, col_tiles, p, my_row, my_col, n_col)
    stacked_tiles = jnp.stack(tiles)
    return stacked_tiles.reshape(1, blocks, 1, points.shape[0], points.shape[0])


def solution(mesh):
    placed = (P("row", None), P("row"), P(), P())
    return jax.shard_map(
        body,
        mesh=mesh,
        in_specs=placed,
        out_specs=P("row", None, "col", None, None),
        check_vma=False,
    )
```

profile of v0, /device:TPU:8, one launch (start us, length us, event | category | flops | bytes accessed | tf_op | source)
XLA Modules:
  0.0 1198.2 jit_solution(10139373326444151370)
XLA Ops:
  6.5 2.5 broadcast_select_fusion.2
  10.4 158.8 %all-reduce.16.cloned.1.call-done = (f32[512,256]{1,0:T(8,128)}, f32[512,256]{1,0:T(8,128)}, f32[512,256]{1,0:T(8,128)}, f32[512,256]{1,0:T(8,128)}) async-done(((f32[512,256]{1,0:T(8,128)}, f32[512,256]{1,0:T(8,128)}, f32[512,256]{1,0:T(8,128)}, f32[512,256]{1,0:T(8,128)}), (f32[512,256]{1,0:T(8,128)}, f32[512,256]{1,0:T(8,128)}, f32[512,256]{1,0:T(8,128)}, ...) | async-done | bytes 2097168 | tf_op jit(solution)/shard_map/psum | solution.py:9
  169.2 1.9 multiply_reduce_fusion.2
  171.1 3.2 fusion.40
  174.3 1.6 copy.61
  175.9 2.2 broadcast_select_fusion.1
  178.3 147.6 %all-reduce.8.cloned.1.call-done = f32[512,512]{0,1:T(8,128)} async-done(((f32[512,512]{0,1:T(8,128)}), f32[512,512]{0,1:T(8,128)}) %all-reduce.8.cloned.1.call-update) | async-done | bytes 1048592 | tf_op jit(solution)/shard_map/psum | solution.py:9
  325.9 1.6 copy.50
  329.9 11.7 cholesky.286
  341.7 9.8 custom-call.27
  354.2 11.7 cholesky.305
  366.1 10.0 custom-call.28
  378.1 11.7 cholesky.326
  389.9 9.8 custom-call.29
  401.4 12.1 %cholesky.343 = f32[128,128]{1,0:T(8,128)S(1)} custom-call(f32[128,128]{1,0:T(8,128)S(1)} %convolution_subtract_fusion.11), custom_call_target="Cholesky" | custom-call | tf_op jit(solution)/shard_map/jit(cholesky)/cholesky | solution.py:27
  419.3 12.3 %while.4 = (s32[]{:T(128)}, f32[512,512]{0,1:T(8,128)}, s32[4,2]{0,1:T(2,128)S(1)}, f32[4,128,128]{2,1,0:T(8,128)S(1)}, s32[]{:T(128)}) while((s32[]{:T(128)}, f32[512,512]{0,1:T(8,128)}, s32[4,2]{0,1:T(2,128)S(1)}, f32[4,128,128]{2,1,0:T(8,128)S(1)}, s32[]{:T(128)}) %tuple.57), condition=%wide.while_cond, body=%wide.while_body.sunk | while | flops 2 | bytes 393329 | solution.py:28
  420.0 2.3 dynamic-slice.12
  423.1 2.3 dynamic-slice.12
  426.2 2.3 dynamic-slice.12
  429.3 2.2 dynamic-slice.12
  431.6 39.3 %custom-call.30 = f32[4,128,128]{1,2,0:T(8,128)S(1)} custom-call(f32[4,128,128]{2,1,0:T(8,128)S(1)} %get-tuple-element.21), custom_call_target="InvertDiagBlocksLowerTriangular" | custom-call | tf_op jit(solution)/shard_map/jit(_solve_triangular)/triangular_solve | solution.py:28
  473.3 1.6 convolution_subtract_fusion.3
  476.1 2.0 convolution_subtract_fusion.2
  479.4 3.2 convolution_subtract_fusion.5
  484.2 2.1 fusion.36
  486.3 62.9 %all-reduce.10.cloned.1.call-done = f32[512,512]{1,0:T(8,128)} async-done(((f32[512,512]{1,0:T(8,128)}), f32[512,512]{1,0:T(8,128)}) %all-reduce.10.cloned.1.call-update) | async-done | bytes 1048592 | tf_op jit(solution)/shard_map/psum | solution.py:9
  549.1 2.5 copy.66
  552.8 2.5 copy.67
  555.4 11.0 all-to-all-start
  566.5 26.7 %all-to-all-done = f32[32,16,512]{2,1,0:T(8,128)S(1)} async-done(((f32[32,16,512]{2,1,0:T(8,128)}), f32[32,16,512]{2,1,0:T(8,128)S(1)}, u32[]{:S(2)}, u32[]{:S(2)}) %all-to-all-start) | async-done | bytes 1048608 | tf_op jit(solution)/shard_map/all_to_all | solution.py:37
  593.9 81.1 %all-gather.5.cloned.1.call-done = f32[4,1,512,512]{3,2,1,0:T(8,128)} async-done(((f32[4,1,16,512]{3,2,1,0:T(8,128)}), f32[4,1,512,512]{3,2,1,0:T(8,128)}) %all-gather.5.cloned.1.call-update) | async-done | bytes 4194320 | tf_op jit(solution)/shard_map/all_gather | solution.py:40
  675.0 5.4 broadcast_select_fusion
  680.7 147.2 %all-reduce.12.cloned.1.call-done = f32[512,512]{0,1:T(8,128)} async-done(((f32[512,512]{0,1:T(8,128)}), f32[512,512]{0,1:T(8,128)}) %all-reduce.12.cloned.1.call-update) | async-done | bytes 1048592 | tf_op jit(solution)/shard_map/psum | solution.py:9
  831.9 11.7 cholesky.358
  843.7 9.8 custom-call.31
  856.2 11.7 cholesky.377
  868.1 10.0 custom-call.32
  880.1 11.7 cholesky.398
  891.9 9.8 custom-call.33
  903.4 12.1 %cholesky.415 = f32[128,128]{1,0:T(8,128)S(1)} custom-call(f32[128,128]{1,0:T(8,128)S(1)} %convolution_subtract_fusion.10), custom_call_target="Cholesky" | custom-call | tf_op jit(solution)/shard_map/jit(cholesky)/cholesky | solution.py:27
  921.9 12.3 %while.5 = (s32[]{:T(128)}, f32[512,512]{0,1:T(8,128)}, s32[4,2]{0,1:T(2,128)S(1)}, f32[4,128,128]{2,1,0:T(8,128)S(1)}, s32[]{:T(128)}) while((s32[]{:T(128)}, f32[512,512]{0,1:T(8,128)}, s32[4,2]{0,1:T(2,128)S(1)}, f32[4,128,128]{2,1,0:T(8,128)S(1)}, s32[]{:T(128)}) %tuple.78), condition=%wide.while_cond.clone, body=%wide.while_body.clone.sunk | while | flops 2 | bytes 393329 | solution.py:28
  922.6 2.3 dynamic-slice.14
  925.7 2.3 dynamic-slice.14
  928.8 2.3 dynamic-slice.14
  931.9 2.2 dynamic-slice.14
  934.2 39.3 %custom-call.34 = f32[4,128,128]{1,2,0:T(8,128)S(1)} custom-call(f32[4,128,128]{2,1,0:T(8,128)S(1)} %get-tuple-element.22), custom_call_target="InvertDiagBlocksLowerTriangular" | custom-call | tf_op jit(solution)/shard_map/jit(_solve_triangular)/triangular_solve | solution.py:28
  980.0 2.3 convolution_subtract_fusion.4
  982.5 1.6 fusion.91
  984.0 2.1 fusion.37
  986.2 62.8 %all-reduce.14.cloned.1.call-done = f32[512,512]{1,0:T(8,128)} async-done(((f32[512,512]{1,0:T(8,128)}), f32[512,512]{1,0:T(8,128)}) %all-reduce.14.cloned.1.call-update) | async-done | bytes 1048592 | tf_op jit(solution)/shard_map/psum | solution.py:9
  1049.0 2.5 copy.82
  1053.1 38.0 %all_to_all.18 = f32[32,16,512]{2,1,0:T(8,128)S(1)} all-to-all(f32[32,16,512]{2,1,0:T(8,128)} %bitcast.160), channel_id=1, replica_groups=mesh['row'=32,'col'=8] {'row'}, dimensions={0} | all-to-all | bytes 2097152 | tf_op jit(solution)/shard_map/all_to_all | solution.py:37
  1093.6 2.6 fusion.11
  1096.2 2.6 fusion.7
  1100.2 3.1 fusion.21
  1103.3 3.2 fusion.26
  1106.5 3.1 fusion.16
  1109.6 63.2 %all-gather.7.cloned.1.call-done = f32[4,1,512,512]{3,2,1,0:T(8,128)} async-done(((f32[4,1,16,512]{3,2,1,0:T(8,128)}), f32[4,1,512,512]{3,2,1,0:T(8,128)}) %all-gather.7.cloned.1.call-update) | async-done | bytes 4194320 | tf_op jit(solution)/shard_map/all_gather | solution.py:40
  1172.8 3.2 fusion.29
  1176.1 3.4 fusion.19
  1179.6 2.0 fusion.24
  1181.6 2.0 fusion.14
  1183.6 2.4 maximum_bitcast_fusion
  1185.9 5.2 copy.94
  (164 shorter events, 52.5 us)
Async XLA Ops:
  6.5 162.6 %copy-start = (f32[512,256]{1,0:T(8,128)S(1)}, f32[512,256]{1,0:T(8,128)}, u32[]{:S(2)}) copy-start(f32[512,256]{1,0:T(8,128)} %param.7) | copy-start | bytes 1572868
  6.5 2.6 copy-start.16
  6.5 162.6 %copy-start.13 = (f32[256]{0:T(256)S(1)}, f32[256]{0:T(256)}, u32[]{:S(2)}) copy-start(f32[256]{0:T(256)} %param.9) | copy-start | bytes 3076
  6.5 162.6 %all-reduce.16.cloned.1.call-start = ((), (), s32[]{:S(2)}) async-start(), calls=%async_computation.8 | async-start | bytes 4194304 | tf_op jit(solution)/shard_map/psum | solution.py:9
  9.0 166.8 %copy-start.14 = (f32[512]{0:T(512)S(1)}, f32[512]{0:T(512)}, u32[]{:S(2)}) copy-start(f32[512]{0:T(512)} %param.8) | copy-start | bytes 6148
  9.1 316.8 %all-reduce.8.cloned.1.call-start = ((), (), s32[]{:S(2)}) async-start(), calls=%async_computation.2 | async-start | bytes 2097152 | tf_op jit(solution)/shard_map/psum | solution.py:9
  178.1 371.0 %all-reduce.10.cloned.1.call-start = ((), (), s32[]{:S(2)}) async-start(), calls=%async_computation.3 | async-start | bytes 2097152 | tf_op jit(solution)/shard_map/psum | solution.py:9
  328.9 1.0 copy-start.6
  471.0 5.2 copy-start.11
  555.4 37.8 %all-to-all-start = ((f32[32,16,512]{2,1,0:T(8,128)}), f32[32,16,512]{2,1,0:T(8,128)S(1)}, u32[]{:S(2)}, u32[]{:S(2)}) async-start(f32[32,16,512]{2,1,0:T(8,128)} %bitcast.14), calls=%async_computation | async-start | bytes 2097152 | tf_op jit(solution)/shard_map/all_to_all | solution.py:37
  566.4 108.6 %all-gather.5.cloned.1.call-start = ((), (), s32[]{:S(2)}) async-start(), calls=%async_computation.6 | async-start | bytes 4325376 | tf_op jit(solution)/shard_map/all_gather | solution.py:40
  593.9 234.0 %all-reduce.12.cloned.1.call-start = ((), (), s32[]{:S(2)}) async-start(), calls=%async_computation.4 | async-start | bytes 2097152 | tf_op jit(solution)/shard_map/psum | solution.py:9
  680.4 299.6 %copy-start.2 = (f32[512,512]{0,1:T(8,128)}, f32[512,512]{0,1:T(8,128)S(1)}, u32[]{:S(2)}) copy-start(f32[512,512]{0,1:T(8,128)S(1)} %get-tuple-element.89) | copy-start | bytes 3145732
  680.5 368.5 %all-reduce.14.cloned.1.call-start = ((), (), s32[]{:S(2)}) async-start(), calls=%async_computation.5 | async-start | bytes 2097152 | tf_op jit(solution)/shard_map/psum | solution.py:9
  830.9 1.0 copy-start.7
  973.5 3.8 copy-start.12
  986.1 186.7 %all-gather.7.cloned.1.call-start = ((), (), s32[]{:S(2)}) async-start(), calls=%async_computation.7 | async-start | bytes 4325376 | tf_op jit(solution)/shard_map/all_gather | solution.py:40
  1051.7 47.1 %copy-start.8 = (f32[512,256]{1,0:T(8,128)S(1)}, f32[512,256]{1,0:T(8,128)}, u32[]{:S(2)}) copy-start(f32[512,256]{1,0:T(8,128)} %get-tuple-element.63) | copy-start | bytes 1572868
  1053.1 47.2 %copy-start.4 = (f32[512,512]{0,1:T(8,128)S(1)}, f32[512,512]{0,1:T(8,128)}, u32[]{:S(2)}) copy-start(f32[512,512]{0,1:T(8,128)} %select_select_fusion.5) | copy-start | bytes 3145732
  1093.6 6.7 copy-start.15
  1096.2 7.1 copy-start.5
  1103.3 69.5 %copy-start.3 = (f32[512,512]{0,1:T(8,128)S(1)}, f32[512,512]{0,1:T(8,128)}, u32[]{:S(2)}) copy-start(f32[512,512]{0,1:T(8,128)} %copy-done.2) | copy-start | bytes 3145732
  1172.8 3.3 copy-start.1
  1172.8 6.7 copy-start.9
  1176.1 5.5 copy-start.10
Sparse Core Ops, SparseCore 0:
  11.2 157.8 all-reduce.15
  178.2 147.6 all-reduce.7
  486.4 62.7 all-reduce.9
  594.0 80.9 all-gather.4
  680.6 147.2 all-reduce.11
  986.3 62.7 all-reduce.13
  1091.8 80.9 all-gather.6
where the time goes:
time: 1200 us
  waiting for transfers between devices  750 us (62%)
  other arithmetic  257 us (21%)
  matrix products  67 us (6%)
  local copies, waits for them, and re-layouts  52.1 us (4%)
  blocking collectives  38 us (3%)
  between operations  22.1 us (2%)
    psum x5, waiting for transfers between devices, broadcast(): return lax.psum(kept, axis)  579 us
    another operation x29, other arithmetic, factor_panel(): lpp = jnp.linalg.cholesky(diag_tile)  159 us
    all_gather x2, waiting for transfers between devices, column_factors(): whole = lax.all_gather(picked, 'row', axis=1, tiled=True)  144 us
    another operation x5, other arithmetic, factor_panel(): solved = jax.scipy.linalg.solve_triangular(lpp, local.T, lower=True).T  80.8 us
    all_to_all x1, blocking collectives, column_factors(): lax.all_to_all(panel, 'row', split_axis=0, concat_axis=0, tiled=True)  38 us
    another operation x49, local copies, waits for them, and re-layouts, factor_panel(): solved = jax.scipy.linalg.solve_triangular(lpp, local.T, lower=True).T  28 us
    all_to_all x1, waiting for transfers between devices, column_factors(): lax.all_to_all(panel, 'row', split_axis=0, concat_axis=0, tiled=True)  26.7 us
    dot_general x8, matrix products, apply_panel(): jnp.dot(panel, col_tiles[k].T, precision=lax.Precision.HIGHEST, preferred...  25.5 us
  transfers between devices with their start and end apart: 8, of which 8 were waited for; matrix products, arithmetic and copies ran while one was open for 1% of the time, Pallas kernels for 0%

commit v1 on v0

--- a/solution.py
+++ b/solution.py
@@ -6,7 +6,7 @@
 
 def broadcast(value, axis, source):
     kept = jnp.where(lax.axis_index(axis) == source, value, 0).astype(value.dtype)
-    return lax.psum(kept, axis)
+    return jnp.sum(lax.all_gather(kept, axis_name=axis), 0)
 
 
 def kernel_tile(xrow, xcol, weights):

time: 1200 us -> 1770 us (1.48)
  waiting for transfers between devices: 750 us -> 1260 us
  other arithmetic: 257 us -> 316 us
    all_gather x0 -> x8, waiting for transfers between devices: none -> 1090 us  [broadcast(): return jnp.sum(lax.all_gather(kept, axis_name=axis), 0)]
    psum x5 -> x0, waiting for transfers between devices: 579 us -> none  [broadcast(): return lax.psum(kept, axis)]
    reduce_sum x0 -> x8, other arithmetic: none -> 58.8 us  [broadcast(): return jnp.sum(lax.all_gather(kept, axis_name=axis), 0)]
    unnamed x34 -> x42, local copies, waits for them, and re-layouts: 2 us -> 26.4 us
  transfers between devices with their start and end apart: 8 -> 11, of which waited for: 8 -> 11; matrix products, arithmetic and copies ran while one was open for 1% -> 2% of each run, Pallas kernels for 0% -> 0%
where the time goes in v1:
time: 1770 us
  waiting for transfers between devices  1260 us (71%)
  other arithmetic  316 us (18%)
  matrix products  61 us (3%)
  local copies, waits for them, and re-layouts  57.3 us (3%)
  blocking collectives  40 us (2%)
  between operations  22.1 us (1%)
    all_gather x8, waiting for transfers between devices, broadcast(): return jnp.sum(lax.all_gather(kept, axis_name=axis), 0)  1090 us
    another operation x29, other arithmetic, factor_panel(): lpp = jnp.linalg.cholesky(diag_tile)  158 us
    all_gather x2, waiting for transfers between devices, column_factors(): whole = lax.all_gather(picked, 'row', axis=1, tiled=True)  135 us
    another operation x5, other arithmetic, factor_panel(): solved = jax.scipy.linalg.solve_triangular(lpp, local.T, lower=True).T  83 us
    reduce_sum x8, other arithmetic, broadcast(): return jnp.sum(lax.all_gather(kept, axis_name=axis), 0)  58.8 us
    all_to_all x1, blocking collectives, column_factors(): lax.all_to_all(panel, 'row', split_axis=0, concat_axis=0, tiled=True)  40 us
  transfers between devices with their start and end apart: 11, of which 11 were waited for; matrix products, arithmetic and copies ran while one was open for 2% of the time, Pallas kernels for 0%

profile of v1, /device:TPU:8, one launch (start us, length us, event | category | flops | bytes accessed | tf_op | source)
XLA Modules:
  0.0 1765.6 jit_solution(14467153588467023790)
XLA Ops:
  6.5 2.4 broadcast_select_fusion.2
  12.4 140.1 %all-gather.21.cloned.1.call-done = f32[16384,256]{1,0:T(8,128)} async-done(((f32[512,256]{1,0:T(8,128)}), f32[16384,256]{1,0:T(8,128)}) %all-gather.21.cloned.1.call-update) | async-done | bytes 16777232 | tf_op jit(solution)/shard_map/all_gather | solution.py:9
  152.5 6.9 reduce_sum.130
  161.8 130.0 %all-gather.39.cloned.1.call-done = f32[16384,256]{1,0:T(8,128)} async-done(((f32[512,256]{1,0:T(8,128)}), f32[16384,256]{1,0:T(8,128)}) %all-gather.39.cloned.1.call-update) | async-done | bytes 16777232 | tf_op jit(solution)/shard_map/all_gather | solution.py:9
  291.9 6.9 reduce_sum.140
  298.8 132.5 %all-gather.35.cloned.1.call-done = f32[16384,256]{1,0:T(8,128)} async-done(((f32[512,256]{1,0:T(8,128)}), f32[16384,256]{1,0:T(8,128)}) %all-gather.35.cloned.1.call-update) | async-done | bytes 16777232 | tf_op jit(solution)/shard_map/all_gather | solution.py:9
  431.2 6.9 reduce_sum.136
  438.1 132.3 %all-gather.37.cloned.1.call-done = f32[16384,256]{1,0:T(8,128)} async-done(((f32[512,256]{1,0:T(8,128)}), f32[16384,256]{1,0:T(8,128)}) %all-gather.37.cloned.1.call-update) | async-done | bytes 16777232 | tf_op jit(solution)/shard_map/all_gather | solution.py:9
  570.5 6.9 reduce_sum.138
  579.1 3.9 broadcast_select_fusion.1
  583.0 230.1 %all-gather.23.cloned.1.call-done = f32[16384,512]{1,0:T(8,128)} async-done(((f32[512,512]{1,0:T(8,128)}), f32[16384,512]{1,0:T(8,128)}) %all-gather.23.cloned.1.call-update) | async-done | bytes 33554448 | tf_op jit(solution)/shard_map/all_gather | solution.py:9
  813.1 12.4 reduce_sum.132
  829.3 11.7 cholesky.286
  841.1 9.8 custom-call.27
  853.6 11.7 cholesky.305
  865.3 10.2 custom-call.28
  877.1 11.7 cholesky.326
  889.5 9.8 custom-call.29
  900.7 11.7 cholesky.343
  917.5 11.3 while.4
  918.1 2.2 bitcast_dynamic-update-slice_fusion.4
  921.0 2.2 bitcast_dynamic-update-slice_fusion.4
  923.8 2.2 bitcast_dynamic-update-slice_fusion.4
  926.7 2.1 bitcast_dynamic-update-slice_fusion.4
  929.5 40.1 %custom-call.30 = f32[4,128,128]{1,2,0:T(8,128)S(1)} custom-call(f32[4,128,128]{2,1,0:T(8,128)} %copy-done.15), custom_call_target="InvertDiagBlocksLowerTriangular" | custom-call | tf_op jit(solution)/shard_map/jit(_solve_triangular)/triangular_solve | solution.py:28
  973.6 1.7 convolution_subtract_fusion.5
  977.0 48.7 %all-gather.25.cloned.1.call-done = f32[4096,512]{0,1:T(8,128)} async-done(((f32[512,512]{0,1:T(8,128)}), f32[4096,512]{0,1:T(8,128)}) %all-gather.25.cloned.1.call-update) | async-done | bytes 8388624 | tf_op jit(solution)/shard_map/all_gather | solution.py:9
  1025.6 11.5 copy.20
  1037.1 3.5 bitcast_reduce_fusion.1
  1043.0 11.1 all-to-all-start
  1054.2 29.0 %all-to-all-done = f32[32,16,512]{2,1,0:T(8,128)S(1)} async-done(((f32[32,16,512]{2,1,0:T(8,128)}), f32[32,16,512]{2,1,0:T(8,128)S(1)}, u32[]{:S(2)}, u32[]{:S(2)}) %all-to-all-start) | async-done | bytes 1048608 | tf_op jit(solution)/shard_map/all_to_all | solution.py:37
  1083.9 78.1 %all-gather.27.cloned.1.call-done = f32[4,1,512,512]{3,2,1,0:T(8,128)} async-done(((f32[4,1,16,512]{3,2,1,0:T(8,128)}), f32[4,1,512,512]{3,2,1,0:T(8,128)}) %all-gather.27.cloned.1.call-update) | async-done | bytes 4194320 | tf_op jit(solution)/shard_map/all_gather | solution.py:40
  1162.0 5.7 broadcast_select_fusion
  1167.8 229.8 %all-gather.29.cloned.1.call-done = f32[16384,512]{1,0:T(8,128)} async-done(((f32[512,512]{1,0:T(8,128)}), f32[16384,512]{1,0:T(8,128)}) %all-gather.29.cloned.1.call-update) | async-done | bytes 33554448 | tf_op jit(solution)/shard_map/all_gather | solution.py:9
  1397.6 12.3 reduce_sum.134
  1411.5 11.7 cholesky.358
  1423.8 9.8 custom-call.31
  1436.3 11.7 cholesky.377
  1448.8 10.0 custom-call.32
  1460.3 11.7 cholesky.398
  1472.8 9.8 custom-call.33
  1484.0 11.7 cholesky.415
  1500.5 11.9 while.5
  1501.2 2.3 bitcast_dynamic-update-slice_fusion.5
  1504.2 2.3 bitcast_dynamic-update-slice_fusion.5
  1507.2 2.3 bitcast_dynamic-update-slice_fusion.5
  1510.2 2.2 bitcast_dynamic-update-slice_fusion.5
  1513.1 40.1 %custom-call.34 = f32[4,128,128]{1,2,0:T(8,128)S(1)} custom-call(f32[4,128,128]{2,1,0:T(8,128)} %copy-done.14), custom_call_target="InvertDiagBlocksLowerTriangular" | custom-call | tf_op jit(solution)/shard_map/jit(_solve_triangular)/triangular_solve | solution.py:28
  1555.6 1.9 convolution_subtract_fusion
  1557.9 2.4 convolution_subtract_fusion.4
  1561.9 48.6 %all-gather.31.cloned.1.call-done = f32[4096,512]{0,1:T(8,128)} async-done(((f32[512,512]{0,1:T(8,128)}), f32[4096,512]{0,1:T(8,128)}) %all-gather.31.cloned.1.call-update) | async-done | bytes 8388624 | tf_op jit(solution)/shard_map/all_gather | solution.py:9
  1610.5 11.5 copy.21
  1622.0 3.1 bitcast_reduce_fusion
  1626.6 40.0 %all_to_all.18 = f32[32,16,512]{2,1,0:T(8,128)S(1)} all-to-all(f32[32,16,512]{2,1,0:T(8,128)S(1)} %bitcast.182), channel_id=1, replica_groups=mesh['row'=32,'col'=8] {'row'}, dimensions={0} | all-to-all | bytes 2097152 | tf_op jit(solution)/shard_map/all_to_all | solution.py:37
  1669.2 2.6 fusion.11
  1674.6 4.6 fusion.21
  1679.2 4.7 fusion.26
  1683.9 4.6 fusion.16
  1688.5 57.0 %all-gather.33.cloned.1.call-done = f32[4,1,512,512]{3,2,1,0:T(8,128)} async-done(((f32[4,1,16,512]{3,2,1,0:T(8,128)}), f32[4,1,512,512]{3,2,1,0:T(8,128)}) %all-gather.33.cloned.1.call-update) | async-done | bytes 4194320 | tf_op jit(solution)/shard_map/all_gather | solution.py:40
  1745.4 3.5 fusion.29
  1748.9 3.2 fusion.19
  1752.1 2.0 fusion.24
  1754.1 2.0 fusion.14
  1756.1 2.5 maximum_bitcast_fusion
  (146 shorter events, 55.7 us)
Async XLA Ops:
  6.5 4.6 copy-start.19
  6.5 145.9 %all-gather.21.cloned.1.call-start = ((), (), s32[]{:S(2)}) async-start(), calls=%async_computation.2 | async-start | bytes 17301504 | tf_op jit(solution)/shard_map/all_gather | solution.py:9
  9.0 282.9 %all-gather.39.cloned.1.call-start = ((), (), s32[]{:S(2)}) async-start(), calls=%async_computation.11 | async-start | bytes 17301504 | tf_op jit(solution)/shard_map/all_gather | solution.py:9
  9.7 421.5 %all-gather.35.cloned.1.call-start = ((), (), s32[]{:S(2)}) async-start(), calls=%async_computation.9 | async-start | bytes 17301504 | tf_op jit(solution)/shard_map/all_gather | solution.py:9
  10.4 560.0 %all-gather.37.cloned.1.call-start = ((), (), s32[]{:S(2)}) async-start(), calls=%async_computation.10 | async-start | bytes 17301504 | tf_op jit(solution)/shard_map/all_gather | solution.py:9
  11.0 802.1 %all-gather.23.cloned.1.call-start = ((), (), s32[]{:S(2)}) async-start(), calls=%async_computation.3 | async-start | bytes 34603008 | tf_op jit(solution)/shard_map/all_gather | solution.py:9
  152.5 6.9 copy-start
  152.5 7.0 copy-start.16
  159.5 139.3 %copy-start.4 = (f32[512,256]{1,0:T(8,128)}, f32[512,256]{1,0:T(8,128)S(1)}, u32[]{:S(2)}) copy-start(f32[512,256]{1,0:T(8,128)S(1)} %reduce_sum.130) | copy-start | bytes 1572868
  438.1 139.2 %copy-start.1 = (f32[512,256]{1,0:T(8,128)}, f32[512,256]{1,0:T(8,128)S(1)}, u32[]{:S(2)}) copy-start(f32[512,256]{1,0:T(8,128)S(1)} %reduce_sum.136) | copy-start | bytes 1572868
  570.5 8.6 copy-start.17
  577.4 248.2 %copy-start.2 = (f32[512,256]{1,0:T(8,128)}, f32[512,256]{1,0:T(8,128)S(1)}, u32[]{:S(2)}) copy-start(f32[512,256]{1,0:T(8,128)S(1)} %reduce_sum.138) | copy-start | bytes 1572868
  583.0 442.7 %all-gather.25.cloned.1.call-start = ((), (), s32[]{:S(2)}) async-start(), calls=%async_computation.4 | async-start | bytes 9437184 | tf_op jit(solution)/shard_map/all_gather | solution.py:9
  828.3 1.0 copy-start.11
  829.3 140.3 %copy-start.9 = (f32[512,512]{1,0:T(8,128)S(1)}, f32[512,512]{1,0:T(8,128)}, u32[]{:S(2)}) copy-start(f32[512,512]{1,0:T(8,128)} %get-tuple-element.73) | copy-start | bytes 3145732
  928.8 0.7 copy-start.15
  1041.9 120.2 %copy-start.8 = (f32[512,512]{1,0:T(8,128)S(1)}, f32[512,512]{1,0:T(8,128)}, u32[]{:S(2)}) copy-start(f32[512,512]{1,0:T(8,128)} %copy.13) | copy-start | bytes 3145732
  1043.0 40.1 %all-to-all-start = ((f32[32,16,512]{2,1,0:T(8,128)}), f32[32,16,512]{2,1,0:T(8,128)S(1)}, u32[]{:S(2)}, u32[]{:S(2)}) async-start(f32[32,16,512]{2,1,0:T(8,128)} %bitcast.16), calls=%async_computation | async-start | bytes 2097152 | tf_op jit(solution)/shard_map/all_to_all | solution.py:37
  1054.2 107.9 %all-gather.27.cloned.1.call-start = ((), (), s32[]{:S(2)}) async-start(), calls=%async_computation.5 | async-start | bytes 4325376 | tf_op jit(solution)/shard_map/all_gather | solution.py:40
  1083.9 313.8 %all-gather.29.cloned.1.call-start = ((), (), s32[]{:S(2)}) async-start(), calls=%async_computation.6 | async-start | bytes 34603008 | tf_op jit(solution)/shard_map/all_gather | solution.py:9
  1167.8 442.7 %all-gather.31.cloned.1.call-start = ((), (), s32[]{:S(2)}) async-start(), calls=%async_computation.7 | async-start | bytes 9437184 | tf_op jit(solution)/shard_map/all_gather | solution.py:9
  1410.5 1.0 copy-start.10
  1411.4 141.8 %copy-start.6 = (f32[512,512]{1,0:T(8,128)S(1)}, f32[512,512]{1,0:T(8,128)}, u32[]{:S(2)}) copy-start(f32[512,512]{1,0:T(8,128)} %get-tuple-element.77) | copy-start | bytes 3145732
  1512.5 0.7 copy-start.14
  1561.9 183.5 %all-gather.33.cloned.1.call-start = ((), (), s32[]{:S(2)}) async-start(), calls=%async_computation.8 | async-start | bytes 4325376 | tf_op jit(solution)/shard_map/all_gather | solution.py:40
  1626.6 45.2 %copy-start.3 = (f32[512,256]{1,0:T(8,128)S(1)}, f32[512,256]{1,0:T(8,128)}, u32[]{:S(2)}) copy-start(f32[512,256]{1,0:T(8,128)} %copy-done.2) | copy-start | bytes 1572868
  1669.2 5.4 copy-start.18
  1679.2 66.2 %copy-start.7 = (f32[512,512]{1,0:T(8,128)S(1)}, f32[512,512]{1,0:T(8,128)}, u32[]{:S(2)}) copy-start(f32[512,512]{1,0:T(8,128)} %get-tuple-element.77) | copy-start | bytes 3145732
  1745.4 3.5 copy-start.5
  1745.4 6.7 copy-start.12
  1748.9 5.2 copy-start.13
Sparse Core Ops, SparseCore 0:
  9.9 142.5 all-gather.20
  155.1 136.7 all-gather.38
  294.5 136.7 all-gather.34
  433.7 136.7 all-gather.36
  583.1 229.9 all-gather.22
  977.1 48.5 all-gather.24
  1084.0 77.9 all-gather.26
  1167.9 229.6 all-gather.28
  1562.0 48.4 all-gather.30
  1667.4 77.9 all-gather.32
